TPU v7x, 256 devices: a whole 4x4x8 slice. The times are simulated.
256 devices in a mesh: sample: 32 (over z, y_hi, core), tensor: 8 (over y_lo, x).
Axes of the slice: x: 4, y: 4 (y_hi: 2, y_lo: 2; y = y_hi * 2 + y_lo), z: 8, core: 2. Of those that a mesh axis runs over, the one named last changes fastest.
Arguments:
- hidden: bfloat16 [8192, 14336], P('sample', 'tensor'), may hold values from -6 to 6
- down_weight: bfloat16 [4096, 14336], P('sample', 'tensor'), may hold values from -0.046875 to 0.046875
- cotangent: bfloat16 [8192, 4096], P('sample'), may hold values from -6 to 6
- scores: int32 [128], P('sample'), may hold values from 0 to 38654
- prompt_ids: int32 [128], P('sample'), may hold values from 0 to 3, as said below
Outputs:
- layer_out: bfloat16 [8192, 4096], P('sample', 'tensor')
- hidden_grad: bfloat16 [8192, 14336], P('sample', 'tensor')
- weight_grad: bfloat16 [4096, 14336], P('sample', 'tensor')
Inputs may be any that keep to these rules, and one draw needn't show every extreme that they name: `prompt_ids`: each prompt id names exactly 32 responses.
All inputs are finite; a program needn't handle non-finite values.
Results may differ from a plain program's by a relative error of at most 0.015.
Values may be sent and summed in bfloat16 or wider, within the bound.
No kernel may reach another device: no remote copies, remote signals or barrier semaphores. Data moves between devices by JAX's collectives and lax.ppermute only.
A program may use at most 128 MiB of HBM per device.

v0:
```python
import math
import jax
import jax.numpy as jnp
from jax import lax
from jax.sharding import Mesh
from jax.sharding import PartitionSpec as P

GROUP = 32
SAMPLE = ("z", "yhi", "core")


def sum_to_bf16(received, axis):
    return jnp.sum(received.astype(jnp.float32), axis=axis).astype(jnp.bfloat16)


def shards(hidden, down_weight, cotangent, scores, prompt_ids):
    samples_here = scores.shape[0]
    n_sample = lax.axis_size(SAMPLE)
    n_z = lax.axis_size("z")
    n_yhi = lax.axis_size("yhi")
    n_core = lax.axis_size("core")
    n_tensor = lax.axis_size("tensor")
    prompts = samples_here * n_sample // GROUP
    packed = jnp.concatenate([scores, prompt_ids])[None, :]
    everything = lax.all_gather(packed, SAMPLE, axis=0, tiled=True)
    all_scores = everything[:, :samples_here].reshape(-1)
    all_ids = everything[:, samples_here:].reshape(-1)
    all_rewards = all_scores.astype(jnp.float32) / 64.0
    all_onehot = all_ids[:, None] == jnp.arange(prompts, dtype=jnp.int32)[None, :]
    peak = jnp.max(jnp.where(all_onehot, all_rewards[:, None], jnp.float32(-1e30)), axis=0)
    shifted = jnp.where(all_onehot, jnp.exp(all_rewards[:, None] - peak[None, :]), 0.0)
    total = jnp.sum(shifted, axis=0)
    log_norm = peak + jnp.log(total)
    rewards = scores.astype(jnp.float32) / 64.0
    onehot = prompt_ids[:, None] == jnp.arange(prompts, dtype=jnp.int32)[None, :]
    sample_norm = jnp.sum(jnp.where(onehot, log_norm[None, :], 0.0), axis=1)
    tokens_here = hidden.shape[0]
    token_weight = jnp.repeat(GROUP * jnp.exp(rewards - sample_norm), tokens_here // samples_here)
    weighted = (cotangent.astype(jnp.float32) * token_weight[:, None]).astype(jnp.bfloat16)
    rows_w = down_weight.shape[0]
    d_all = weighted.shape[1]
    d_half = d_all // n_core
    own_first = lax.axis_index("yhi") == 0
    my_core = lax.axis_index("core")
    swap = [(0, 1), (1, 0)]
    weighted_5 = weighted.reshape(tokens_here, n_z, n_yhi, n_core, rows_w)
    weighted_rel = jnp.where(own_first, weighted_5, jnp.flip(weighted_5, axis=2))
    weighted_mine = lax.dynamic_index_in_dim(weighted_rel, my_core, axis=3, keepdims=False)
    weighted_mine = weighted_mine.reshape(tokens_here, d_half)
    weighted_theirs = lax.dynamic_index_in_dim(weighted_rel, 1 - my_core, axis=3, keepdims=False)
    weighted_recv = lax.ppermute(weighted_theirs.reshape(tokens_here, d_half), "core", swap)
    hidden_recv = lax.ppermute(hidden, "core", swap)
    gathered = jnp.concatenate([down_weight, lax.ppermute(down_weight, "yhi", swap)], axis=0)
    gathered = lax.all_gather(gathered, "z", axis=0, tiled=True)
    scale = 1.0 / math.sqrt(tokens_here * n_sample)
    grad_part = (
        lax.dot_general(
            jnp.concatenate([weighted_mine, weighted_recv], axis=0),
            jnp.concatenate([hidden, hidden_recv], axis=0),
            (((0,), (0,)), ((), ())),
            preferred_element_type=jnp.float32,
        )
        * scale
    ).astype(jnp.bfloat16)
    grad_part = lax.psum_scatter(grad_part, "z", scatter_dimension=0, tiled=True)
    weight_grad = (
        grad_part[:rows_w].astype(jnp.float32)
        + lax.ppermute(grad_part[rows_w:], "yhi", swap).astype(jnp.float32)
    ).astype(jnp.bfloat16)

    def value_of(rows):
        return lax.dot_general(
            rows, gathered, (((1,), (1,)), ((), ())), preferred_element_type=jnp.float32
        ).astype(jnp.bfloat16)

    value_mine = value_of(hidden)
    value_recv = lax.ppermute(value_of(hidden_recv), "core", swap)
    partial_value = jnp.stack([value_mine, value_recv], axis=1)
    partial_value = jnp.where(my_core == 0, partial_value, jnp.flip(partial_value, axis=1))
    partial_value = partial_value.reshape(tokens_here, n_core, n_z, n_yhi, rows_w).transpose(
        0, 2, 3, 1, 4
    )
    partial_value = jnp.where(own_first, partial_value, jnp.flip(partial_value, axis=2)).reshape(
        tokens_here, n_tensor, d_all // n_tensor
    )
    layer_out = sum_to_bf16(lax.all_to_all(partial_value, "tensor", 1, 1, tiled=True), 1)
    grad_for_other = jnp.dot(weighted_recv, gathered, preferred_element_type=jnp.float32)
    hidden_grad = (
        jnp.dot(weighted_mine, gathered, preferred_element_type=jnp.float32)
        + lax.ppermute(grad_for_other, "core", swap)
    ).astype(jnp.bfloat16)
    return (layer_out, hidden_grad, weight_grad)


def solution(mesh):
    n_tensor = mesh.shape["tensor"]
    fine = Mesh(mesh.devices.reshape(-1, 2, 2, n_tensor), ("z", "yhi", "core", "tensor"))
    return jax.shard_map(
        shards,
        mesh=fine,
        in_specs=(P(SAMPLE, "tensor"), P(SAMPLE, "tensor"), P(SAMPLE, None), P(SAMPLE), P(SAMPLE)),
        out_specs=(P(SAMPLE, "tensor"), P(SAMPLE, "tensor"), P(SAMPLE, "tensor")),
        check_vma=False,
    )
```

profile of v0, /device:TPU:2, one launch (start us, length us, event | category | flops | bytes accessed | tf_op | source)
XLA Modules:
  0.0 221.6 jit_solution(11949393025093331972)
XLA Ops:
  7.3 3.3 %collective-permute-start = (bf16[128,1792]{1,0:T(8,128)(2,1)}, bf16[128,1792]{1,0:T(8,128)(2,1)S(1)}, u32[]{:S(2)}, u32[]{:S(2)}) collective-permute-start(bf16[128,1792]{1,0:T(8,128)(2,1)} %param.6), channel_id=1, source_target_pairs={{0,16},{16,0},{1,17},{17,1},{2,18},{18,2},{3,19},{19,3},{4,20},{20... | collective-permute-start | bytes 1376264 | tf_op jit(solution)/shard_map/ppermute | solution.py:53
  10.5 10.8 %collective-permute-done = bf16[128,1792]{1,0:T(8,128)(2,1)S(1)} collective-permute-done((bf16[128,1792]{1,0:T(8,128)(2,1)}, bf16[128,1792]{1,0:T(8,128)(2,1)S(1)}, u32[]{:S(2)}, u32[]{:S(2)}) %collective-permute-start) | collective-permute-done | bytes 458784 | tf_op jit(solution)/shard_map/ppermute | solution.py:53
  21.3 2.0 pad_maximum_fusion.1
  24.8 21.3 %all-reduce = s32[256]{0:T(256)S(1)} all-reduce(s32[256]{0:T(256)S(1)} %add_dynamic-update-slice_fusion), channel_id=2, replica_groups=mesh['z'=8,'yhi'=2,'core'=2,'tensor'=8] {'z','yhi','core'}, use_global_device_ids=true, to_apply=%add | all-reduce | flops 256 | bytes 2048
  47.2 2.5 %copy.26 = bf16[256,4096]{0,1:T(8,128)(2,1)} copy(bf16[256,4096]{1,0:T(8,128)(2,1)S(1)} %copy-done.1) | data formatting | bytes 4194304 | tf_op args[2]
  49.8 2.0 multiply_convert_fusion.1
  51.8 3.2 %copy.28 = bf16[256,8,2,2,128]{4,1,3,2,0:T(8,128)(2,1)} copy(bf16[256,8,2,2,128]{0,4,3,2,1:T(8,128)(2,1)S(1)} %bitcast.22) | data formatting | bytes 4194304 | tf_op jit(solution)/shard_map/reshape | solution.py:46
  55.0 2.8 %reverse_select_fusion = bf16[256,8,2,2,128]{4,1,3,2,0:T(8,128)(2,1)S(1)} fusion(bf16[256,8,2,2,128]{4,1,3,2,0:T(8,128)(2,1)} %copy.28, pred[]{:T(512)S(6)} %eq.34), kind=kLoop, calls=%fused_computation.2 | loop fusion | flops 1048576 | bytes 4194305 | tf_op jit(solution)/shard_map/jit(_where)/select_n | solution.py:47
  61.0 3.0 %collective-permute-done.1 = bf16[256,1792]{1,0:T(8,128)(2,1)} collective-permute-done((bf16[256,1792]{1,0:T(8,128)(2,1)}, bf16[256,1792]{1,0:T(8,128)(2,1)}, u32[]{:S(2)}, u32[]{:S(2)}) %collective-permute-start.1) | collective-permute-done | bytes 917536 | tf_op jit(solution)/shard_map/ppermute | solution.py:52
  64.1 7.5 %multiply_convert_fusion = bf16[2048,1792]{1,0:T(8,128)(2,1)} fusion(bf16[256,2048]{0,1:T(8,128)(2,1)S(1)} %collective-permute-done.3, bf16[256,2048]{0,1:T(8,128)(2,1)S(1)} %bitcast.26, bf16[256,1792]{1,0:T(8,128)(2,1)} %collective-permute-done.1, bf16[256,1792]{1,0:T(8,128)(2,1)} %param.5), kind=kOutput, calls=%fused_computation | convolution fusion | flops 3773300736 | bytes 11272192 | tf_op jit(solution)/shard_map/dot_general | solution.py:57
  71.6 39.2 %all-gather.3.cloned.1.call-done = bf16[2048,1792]{1,0:T(8,128)(2,1)} async-done(((bf16[256,1792]{1,0:T(8,128)(2,1)}), bf16[2048,1792]{1,0:T(8,128)(2,1)}) %all-gather.3.cloned.1.call-update) | async-done | bytes 7340048 | tf_op jit(solution)/shard_map/all_gather | solution.py:54
  110.9 5.5 %fusion.2 = bf16[256,2048]{0,1:T(8,128)(2,1)S(1)} fusion(bf16[2048,1792]{1,0:T(8,128)(2,1)} %all-gather.3.cloned.1.call-done, bf16[256,1792]{1,0:T(8,128)(2,1)} %collective-permute-done.1), kind=kOutput, calls=%fused_computation.10 | convolution fusion | flops 1879572480 | bytes 9306112 | tf_op jit(solution)/shard_map/dot_general | solution.py:72
  116.5 3.3 %fusion.11 = f32[256,1792]{1,0:T(8,128)} fusion(bf16[256,2048]{0,1:T(8,128)(2,1)S(1)} %collective-permute-done.3, bf16[2048,1792]{1,0:T(8,128)(2,1)S(1)} %copy-done), kind=kOutput, calls=%fused_computation.33 | convolution fusion | flops 1879048192 | bytes 10223616 | tf_op jit(solution)/shard_map/dot_general | solution.py:87
  120.3 3.4 %fusion.1 = bf16[256,1,2048]{0,2,1:T(8,128)(2,1)S(1)} fusion(bf16[2048,1792]{1,0:T(8,128)(2,1)S(1)} %copy-done, bf16[256,1792]{1,0:T(8,128)(2,1)} %param.5), kind=kOutput, calls=%fused_computation.9 | convolution fusion | flops 1879572480 | bytes 9306112 | tf_op jit(solution)/shard_map/dot_general | solution.py:72
  124.4 3.2 %copy.24 = bf16[256,2,8,2,128]{4,2,1,3,0:T(8,128)(2,1)} copy(bf16[256,2,8,2,128]{0,4,3,2,1:T(8,128)(2,1)S(1)} %bitcast.23) | data formatting | bytes 4194304 | tf_op jit(solution)/shard_map/reshape | solution.py:80
  127.6 2.8 %reverse_select_fusion.1 = bf16[256,8,2,2,128]{4,1,3,2,0:T(8,128)(2,1)S(1)} fusion(bf16[256,8,2,2,128]{4,1,3,2,0:T(8,128)(2,1)} %bitcast.24, pred[]{:T(512)S(6)} %eq.34), kind=kLoop, calls=%fused_computation.3 | loop fusion | flops 1048576 | bytes 4194305 | tf_op jit(solution)/shard_map/jit(_where)/select_n | solution.py:83
  130.4 2.0 copy.25
  132.4 5.7 %all-to-all-start = ((bf16[256,8,512]{2,0,1:T(8,128)(2,1)}), bf16[256,8,512]{2,0,1:T(8,128)(2,1)S(1)}, u32[]{:S(2)}, u32[]{:S(2)}) async-start(bf16[256,8,512]{2,0,1:T(8,128)(2,1)} %copy.25), calls=%async_computation | async-start | bytes 4194304 | tf_op jit(solution)/shard_map/all_to_all | solution.py:86
  138.1 58.9 %reduce-scatter.2.cloned.1.call-done = bf16[256,1792]{1,0:T(8,128)(2,1)} async-done(((bf16[2048,1792]{1,0:T(8,128)(2,1)}), bf16[256,1792]{1,0:T(8,128)(2,1)}) %reduce-scatter.2.cloned.1.call-update) | async-done | bytes 917520 | tf_op jit(solution)/shard_map/reduce_scatter | solution.py:65
  197.0 1.8 slice.19
  198.8 3.0 %collective-permute-start.5 = (bf16[128,1792]{1,0:T(8,128)(2,1)}, bf16[128,1792]{1,0:T(8,128)(2,1)}, u32[]{:S(2)}, u32[]{:S(2)}) collective-permute-start(bf16[128,1792]{1,0:T(8,128)(2,1)} %slice.19), channel_id=1, source_target_pairs={{0,16},{16,0},{1,17},{17,1},{2,18},{18,2},{3,19},{19,3},{4,20},{20... | collective-permute-start | bytes 1376264 | tf_op jit(solution)/shard_map/ppermute | solution.py:68
  201.8 6.6 %fusion = bf16[256,1792]{1,0:T(8,128)(2,1)} fusion(f32[256,1792]{1,0:T(8,128)} %collective-permute-done.4, bf16[256,2048]{0,1:T(8,128)(2,1)S(1)} %bitcast.27, bf16[2048,1792]{1,0:T(8,128)(2,1)} %all-gather.3.cloned.1.call-done), kind=kOutput, calls=%fused_computation.8 | convolution fusion | flops 1879965696 | bytes 11141120 | tf_op jit(solution)/shard_map/dot_general | solution.py:89
  209.5 3.3 %collective-permute-done.5 = bf16[128,1792]{1,0:T(8,128)(2,1)} collective-permute-done((bf16[128,1792]{1,0:T(8,128)(2,1)}, bf16[128,1792]{1,0:T(8,128)(2,1)}, u32[]{:S(2)}, u32[]{:S(2)}) %collective-permute-start.5) | collective-permute-done | bytes 458784 | tf_op jit(solution)/shard_map/ppermute | solution.py:68
  212.8 1.9 add_convert_fusion
  (45 shorter events, 7.5 us)
Async XLA Ops:
  7.2 16.2 %copy-start.5 = (u32[256]{0:T(256)S(1)}, u32[256]{0:T(256)}, u32[]{:S(2)}) copy-start(u32[256]{0:T(256)} %constant.44) | copy-start | bytes 3076
  7.2 17.5 %copy-start.4 = (s32[4]{0:T(128)S(1)}, s32[4]{0:T(128)}, u32[]{:S(2)}) copy-start(s32[4]{0:T(128)} %param.8) | copy-start | bytes 52
  7.2 17.5 %copy-start.3 = (s32[4]{0:T(128)S(1)}, s32[4]{0:T(128)}, u32[]{:S(2)}) copy-start(s32[4]{0:T(128)} %param.9) | copy-start | bytes 52
  7.2 40.0 %copy-start.1 = (bf16[256,4096]{1,0:T(8,128)(2,1)S(1)}, bf16[256,4096]{1,0:T(8,128)(2,1)}, u32[]{:S(2)}) copy-start(bf16[256,4096]{1,0:T(8,128)(2,1)} %param.7) | copy-start | bytes 6291460
  7.2 103.7 %all-gather.3.cloned.1.call-start = ((), (), s32[]{:S(2)}) async-start(), calls=%async_computation.2 | async-start | bytes 8257536 | tf_op jit(solution)/shard_map/all_gather | solution.py:54
  7.3 14.1 %collective-permute-start = (bf16[128,1792]{1,0:T(8,128)(2,1)}, bf16[128,1792]{1,0:T(8,128)(2,1)S(1)}, u32[]{:S(2)}, u32[]{:S(2)}) collective-permute-start(bf16[128,1792]{1,0:T(8,128)(2,1)} %param.6), channel_id=1, source_target_pairs={{0,16},{16,0},{1,17},{17,1},{2,18},{18,2},{3,19},{19,3},{4,20},{20... | collective-permute-start | bytes 1376264 | tf_op jit(solution)/shard_map/ppermute | solution.py:53
  23.3 173.7 %reduce-scatter.2.cloned.1.call-start = ((), (), s32[]{:S(2)}) async-start(), calls=%async_computation.3 | async-start | bytes 8257536 | tf_op jit(solution)/shard_map/reduce_scatter | solution.py:65
  59.7 4.3 %collective-permute-start.3 = (bf16[256,2048]{0,1:T(8,128)(2,1)}, bf16[256,2048]{0,1:T(8,128)(2,1)S(1)}, u32[]{:S(2)}, u32[]{:S(2)}) collective-permute-start(bf16[256,2048]{0,1:T(8,128)(2,1)} %bitcast.10), channel_id=1, source_target_pairs={{0,8},{8,0},{1,9},{9,1},{2,10},{10,2},{3,11},{11,3},{4,12},{12,4},... | collective-permute-start | bytes 3145736 | tf_op jit(solution)/shard_map/ppermute | solution.py:51
  59.7 4.3 %collective-permute-start.1 = (bf16[256,1792]{1,0:T(8,128)(2,1)}, bf16[256,1792]{1,0:T(8,128)(2,1)}, u32[]{:S(2)}, u32[]{:S(2)}) collective-permute-start(bf16[256,1792]{1,0:T(8,128)(2,1)} %param.5), channel_id=1, source_target_pairs={{0,8},{8,0},{1,9},{9,1},{2,10},{10,2},{3,11},{11,3},{4,12},{12,4},... | collective-permute-start | bytes 2752520 | tf_op jit(solution)/shard_map/ppermute | solution.py:52
  110.9 5.6 %copy-start = (bf16[2048,1792]{1,0:T(8,128)(2,1)S(1)}, bf16[2048,1792]{1,0:T(8,128)(2,1)}, u32[]{:S(2)}) copy-start(bf16[2048,1792]{1,0:T(8,128)(2,1)} %all-gather.3.cloned.1.call-done) | copy-start | bytes 22020100
  116.4 7.3 %collective-permute-start.2 = (bf16[256,2048]{0,1:T(8,128)(2,1)S(1)}, bf16[256,2048]{0,1:T(8,128)(2,1)S(1)}, u32[]{:S(2)}, u32[]{:S(2)}) collective-permute-start(bf16[256,2048]{0,1:T(8,128)(2,1)S(1)} %fusion.2), channel_id=1, source_target_pairs={{0,8},{8,0},{1,9},{9,1},{2,10},{10,2},{3,11},{11,3},{4,12},{12,4},... | collective-permute-start | bytes 3145736 | tf_op jit(solution)/shard_map/ppermute | solution.py:77
  119.9 82.0 %collective-permute-start.4 = (f32[256,1792]{1,0:T(8,128)}, f32[256,1792]{1,0:T(8,128)}, u32[]{:S(2)}, u32[]{:S(2)}) collective-permute-start(f32[256,1792]{1,0:T(8,128)} %fusion.11), channel_id=1, source_target_pairs={{0,8},{8,0},{1,9},{9,1},{2,10},{10,2},{3,11},{11,3},{4,12},{12,4},... | collective-permute-start | bytes 5505032 | tf_op jit(solution)/shard_map/ppermute | solution.py:90
  132.4 76.1 %all-to-all-start = ((bf16[256,8,512]{2,0,1:T(8,128)(2,1)}), bf16[256,8,512]{2,0,1:T(8,128)(2,1)S(1)}, u32[]{:S(2)}, u32[]{:S(2)}) async-start(bf16[256,8,512]{2,0,1:T(8,128)(2,1)} %copy.25), calls=%async_computation | async-start | bytes 4194304 | tf_op jit(solution)/shard_map/all_to_all | solution.py:86
  198.8 14.0 %collective-permute-start.5 = (bf16[128,1792]{1,0:T(8,128)(2,1)}, bf16[128,1792]{1,0:T(8,128)(2,1)}, u32[]{:S(2)}, u32[]{:S(2)}) collective-permute-start(bf16[128,1792]{1,0:T(8,128)(2,1)} %slice.19), channel_id=1, source_target_pairs={{0,16},{16,0},{1,17},{17,1},{2,18},{18,2},{3,19},{19,3},{4,20},{20... | collective-permute-start | bytes 1376264 | tf_op jit(solution)/shard_map/ppermute | solution.py:68
  208.4 4.4 %copy-start.2 = (bf16[256,1792]{1,0:T(8,128)(2,1)S(1)}, bf16[256,1792]{1,0:T(8,128)(2,1)}, u32[]{:S(2)}) copy-start(bf16[256,1792]{1,0:T(8,128)(2,1)} %reduce-scatter.2.cloned.1.call-done) | copy-start | bytes 2752516
Sparse Core Ops, SparseCore 0:
  23.5 87.3 all-gather.2
  113.4 83.5 reduce-scatter.1
where the time goes:
time: 222 us
  waiting for transfers between devices  115 us (52%)
  matrix products  26.4 us (12%)
  blocking collectives  21.3 us (10%)
  local copies, waits for them, and re-layouts  16.6 us (7%)
  between operations  14.9 us (7%)
  other arithmetic  13.9 us (6%)
  starting transfers between devices  13.2 us (6%)
    reduce_scatter x1, waiting for transfers between devices, shards(): lax.psum_scatter(grad_part, 'z', scatter_dimension=0, tiled=True)  58.9 us
    all_gather x1, waiting for transfers between devices, shards(): gathered = lax.all_gather(gathered, 'z', axis=0, tiled=True)  39.2 us
    unnamed x1, blocking collectives  21.3 us
    ppermute x1, waiting for transfers between devices, shards(): lax.ppermute(down_weight, 'yhi', swap)  10.8 us
    dot_general x2, matrix products, value_of(): lax.dot_general(rows, gathered, (((1,), (1,)), ((), ())), preferred_eleme...  8.89 us
    dot_general x1, matrix products, shards(): lax.dot_general(jnp.concatenate([weighted_mine, weighted_recv], axis=0),...  7.53 us
    dot_general x1, matrix products, shards(): jnp.dot(weighted_mine, gathered, preferred_element_type=jnp.float32)  6.61 us
    all_to_all x1, starting transfers between devices, shards(): lax.all_to_all(partial_value, 'tensor', 1, 1, tiled=True)  5.7 us
  transfers between devices with their start and end apart: 9, of which 5 were waited for; matrix products, arithmetic and copies ran while one was open for 24% of the time, Pallas kernels for 0%

commit v1 on v0

--- a/solution.py
+++ b/solution.py
@@ -51,7 +51,9 @@
     weighted_recv = lax.ppermute(weighted_theirs.reshape(tokens_here, d_half), "core", swap)
     hidden_recv = lax.ppermute(hidden, "core", swap)
     gathered = jnp.concatenate([down_weight, lax.ppermute(down_weight, "yhi", swap)], axis=0)
-    gathered = lax.all_gather(gathered, "z", axis=0, tiled=True)
+    gathered = jnp.concatenate(
+        lax.all_to_all(jnp.stack([gathered] * lax.axis_size("z")), "z", 0, 0), axis=0
+    )
     scale = 1.0 / math.sqrt(tokens_here * n_sample)
     grad_part = (
         lax.dot_general(

time: 222 us -> 348 us (1.57)
  waiting for transfers between devices: 115 us -> 228 us
  starting transfers between devices: 13.2 us -> 18.5 us
  local copies, waits for them, and re-layouts: 16.6 us -> 21.9 us
  matrix products: 26.4 us -> 31.4 us
  other arithmetic: 13.9 us -> 10.1 us
    all_to_all x0 -> x1, waiting for transfers between devices: none -> 202 us  [shards(): lax.all_to_all(jnp.stack([gathered] * lax.axis_size('z')), 'z', 0, 0)]
    reduce_scatter x1, waiting for transfers between devices: 58.9 us -> 0.01 us  [shards(): lax.psum_scatter(grad_part, 'z', scatter_dimension=0, tiled=True)]
    all_gather x1 -> x0, waiting for transfers between devices: 39.2 us -> none  [shards(): gathered = lax.all_gather(gathered, 'z', axis=0, tiled=True)]
    all_to_all x1, waiting for transfers between devices: 0.01 us -> 15.5 us  [shards(): lax.all_to_all(partial_value, 'tensor', 1, 1, tiled=True)]
    ppermute x1, waiting for transfers between devices: 10.8 us -> 0.01 us  [shards(): lax.ppermute(down_weight, 'yhi', swap)]
    all_to_all x0 -> x1, starting transfers between devices: none -> 4.85 us  [shards(): lax.all_to_all(jnp.stack([gathered] * lax.axis_size('z')), 'z', 0, 0)]
    ppermute x1, waiting for transfers between devices: 3.33 us -> 7.98 us  [shards(): lax.ppermute(grad_part[rows_w:], 'yhi', swap).astype(jnp.float32)]
    another operation x0 -> x1, local copies, waits for them, and re-layouts: none -> 3.51 us  [shards(): jnp.stack([gathered] * lax.axis_size('z'))]
  transfers between devices with their start and end apart: 9 -> 9, of which waited for: 5 -> 4; matrix products, arithmetic and copies ran while one was open for 24% -> 17% of each run, Pallas kernels for 0% -> 0%
where the time goes in v1:
time: 348 us
  waiting for transfers between devices  228 us (66%)
  matrix products  31.4 us (9%)
  blocking collectives  22.6 us (6%)
  local copies, waits for them, and re-layouts  21.9 us (6%)
  starting transfers between devices  18.5 us (5%)
  between operations  14.8 us (4%)
  other arithmetic  10.1 us (3%)
    all_to_all x1, waiting for transfers between devices, shards(): lax.all_to_all(jnp.stack([gathered] * lax.axis_size('z')), 'z', 0, 0)  202 us
    unnamed x1, blocking collectives  22.6 us
    all_to_all x1, waiting for transfers between devices, shards(): lax.all_to_all(partial_value, 'tensor', 1, 1, tiled=True)  15.5 us
    dot_general x2, matrix products, value_of(): lax.dot_general(rows, gathered, (((1,), (1,)), ((), ())), preferred_eleme...  10.8 us
    ppermute x1, waiting for transfers between devices, shards(): lax.ppermute(grad_part[rows_w:], 'yhi', swap).astype(jnp.float32)  7.98 us
    dot_general x1, matrix products, shards(): lax.dot_general(jnp.concatenate([weighted_mine, weighted_recv], axis=0),...  7.46 us
  transfers between devices with their start and end apart: 9, of which 4 were waited for; matrix products, arithmetic and copies ran while one was open for 17% of the time, Pallas kernels for 0%

profile of v1, /device:TPU:2, one launch (start us, length us, event | category | flops | bytes accessed | tf_op | source)
XLA Modules:
  0.0 347.7 jit_solution(126594929527683922)
XLA Ops:
  7.2 3.3 collective-permute-start
  13.2 22.6 %all-reduce = s32[256]{0:T(256)S(1)} all-reduce(s32[256]{0:T(256)S(1)} %add_dynamic-update-slice_fusion), channel_id=2, replica_groups=mesh['z'=8,'yhi'=2,'core'=2,'tensor'=8] {'z','yhi','core'}, use_global_device_ids=true, to_apply=%add | all-reduce | flops 256 | bytes 2048
  36.0 3.3 copy.26
  40.3 3.5 %stack.8 = bf16[8,256,1792]{2,1,0:T(8,128)(2,1)} broadcast(bf16[256,1792]{1,0:T(8,128)(2,1)S(1)} %pad_maximum_fusion.1), dimensions={1,2} | broadcast | bytes 8257536 | tf_op jit(solution)/shard_map/stack | solution.py:55
  43.8 4.8 %all-to-all-start = ((bf16[8,256,1792]{2,1,0:T(8,128)(2,1)}), bf16[8,256,1792]{2,1,0:T(8,128)(2,1)}, u32[]{:S(2)}, u32[]{:S(2)}) async-start(bf16[8,256,1792]{2,1,0:T(8,128)(2,1)} %stack.8), calls=%async_computation | async-start | bytes 14680064 | tf_op jit(solution)/shard_map/all_to_all | solution.py:55
  48.7 1.8 multiply_convert_fusion.1
  50.5 3.5 copy.28
  54.9 1.6 copy.30
  57.8 3.0 collective-permute-done.1
  60.8 7.5 %multiply_convert_fusion = bf16[2048,1792]{1,0:T(8,128)(2,1)} fusion(bf16[256,2048]{0,1:T(8,128)(2,1)S(1)} %collective-permute-done.3, bf16[256,2048]{0,1:T(8,128)(2,1)S(1)} %bitcast.27, bf16[256,1792]{1,0:T(8,128)(2,1)} %collective-permute-done.1, bf16[256,1792]{1,0:T(8,128)(2,1)} %param.5), kind=kOutput, calls=%fused_computation | convolution fusion | flops 3773300736 | bytes 11272192 | tf_op jit(solution)/shard_map/dot_general | solution.py:59
  68.3 201.8 %all-to-all-done = bf16[8,256,1792]{2,1,0:T(8,128)(2,1)} async-done(((bf16[8,256,1792]{2,1,0:T(8,128)(2,1)}), bf16[8,256,1792]{2,1,0:T(8,128)(2,1)}, u32[]{:S(2)}, u32[]{:S(2)}) %all-to-all-start) | async-done | bytes 7340064 | tf_op jit(solution)/shard_map/all_to_all | solution.py:55
  270.1 5.5 %fusion.1 = bf16[256,2048]{0,1:T(8,128)(2,1)S(1)} fusion(bf16[2048,1792]{1,0:T(8,128)(2,1)} %bitcast, bf16[256,1792]{1,0:T(8,128)(2,1)} %collective-permute-done.1), kind=kOutput, calls=%fused_computation.8 | convolution fusion | flops 1879572480 | bytes 9306112 | tf_op jit(solution)/shard_map/dot_general | solution.py:74
  275.8 6.5 %fusion.10 = f32[256,1792]{1,0:T(8,128)} fusion(bf16[256,2048]{0,1:T(8,128)(2,1)S(1)} %collective-permute-done.3, bf16[2048,1792]{1,0:T(8,128)(2,1)} %bitcast), kind=kOutput, calls=%fused_computation.32 | convolution fusion | flops 1879048192 | bytes 10223616 | tf_op jit(solution)/shard_map/dot_general | solution.py:89
  282.8 5.4 %fusion = bf16[256,1,2048]{0,2,1:T(8,128)(2,1)S(1)} fusion(bf16[2048,1792]{1,0:T(8,128)(2,1)} %bitcast, bf16[256,1792]{1,0:T(8,128)(2,1)} %param.5), kind=kOutput, calls=%fused_computation.7 | convolution fusion | flops 1879572480 | bytes 9306112 | tf_op jit(solution)/shard_map/dot_general | solution.py:74
  288.9 3.2 copy.24
  292.1 2.8 reverse_select_fusion.1
  294.8 2.1 copy.25
  296.9 6.0 %all-to-all-start.1 = ((bf16[256,8,512]{2,0,1:T(8,128)(2,1)}), bf16[256,8,512]{2,0,1:T(8,128)(2,1)S(1)}, u32[]{:S(2)}, u32[]{:S(2)}) async-start(bf16[256,8,512]{2,0,1:T(8,128)(2,1)} %copy.25), calls=%async_computation.1 | async-start | bytes 4194304 | tf_op jit(solution)/shard_map/all_to_all | solution.py:88
  302.9 1.8 slice.19
  304.7 3.2 collective-permute-start.5
  307.9 6.6 %add_convert_fusion = bf16[256,1792]{1,0:T(8,128)(2,1)} fusion(f32[256,1792]{1,0:T(8,128)} %collective-permute-done.4, bf16[256,2048]{0,1:T(8,128)(2,1)S(1)} %bitcast.28, bf16[2048,1792]{1,0:T(8,128)(2,1)} %bitcast), kind=kOutput, calls=%fused_computation.16 | convolution fusion | flops 1879965696 | bytes 11141120 | tf_op jit(solution)/shard_map/dot_general | solution.py:91
  314.5 15.5 %all-to-all-done.1 = bf16[256,8,512]{2,0,1:T(8,128)(2,1)S(1)} async-done(((bf16[256,8,512]{2,0,1:T(8,128)(2,1)}), bf16[256,8,512]{2,0,1:T(8,128)(2,1)S(1)}, u32[]{:S(2)}, u32[]{:S(2)}) %all-to-all-start.1) | async-done | bytes 2097184 | tf_op jit(solution)/shard_map/all_to_all | solution.py:88
  331.0 8.0 %collective-permute-done.5 = bf16[128,1792]{1,0:T(8,128)(2,1)} collective-permute-done((bf16[128,1792]{1,0:T(8,128)(2,1)}, bf16[128,1792]{1,0:T(8,128)(2,1)}, u32[]{:S(2)}, u32[]{:S(2)}) %collective-permute-start.5) | collective-permute-done | bytes 458784 | tf_op jit(solution)/shard_map/ppermute | solution.py:70
  339.0 1.9 add_convert_fusion.1
  (41 shorter events, 7.9 us)
Async XLA Ops:
  7.2 33.1 %collective-permute-start = (bf16[128,1792]{1,0:T(8,128)(2,1)}, bf16[128,1792]{1,0:T(8,128)(2,1)S(1)}, u32[]{:S(2)}, u32[]{:S(2)}) collective-permute-start(bf16[128,1792]{1,0:T(8,128)(2,1)} %param.6), channel_id=1, source_target_pairs={{0,16},{16,0},{1,17},{17,1},{2,18},{18,2},{3,19},{19,3},{4,20},{20... | collective-permute-start | bytes 1376264 | tf_op jit(solution)/shard_map/ppermute | solution.py:53
  36.0 3.9 %copy-start.2 = (s32[4]{0:T(128)S(1)}, s32[4]{0:T(128)}, u32[]{:S(2)}) copy-start(s32[4]{0:T(128)} %param.9) | copy-start | bytes 52
  36.0 4.1 %copy-start.3 = (s32[4]{0:T(128)S(1)}, s32[4]{0:T(128)}, u32[]{:S(2)}) copy-start(s32[4]{0:T(128)} %param.8) | copy-start | bytes 52
  36.0 4.3 %copy-start.1 = (bf16[128,1792]{1,0:T(8,128)(2,1)S(1)}, bf16[128,1792]{1,0:T(8,128)(2,1)}, u32[]{:S(2)}) copy-start(bf16[128,1792]{1,0:T(8,128)(2,1)} %param.6) | copy-start | bytes 1376260
  43.8 226.3 %all-to-all-start = ((bf16[8,256,1792]{2,1,0:T(8,128)(2,1)}), bf16[8,256,1792]{2,1,0:T(8,128)(2,1)}, u32[]{:S(2)}, u32[]{:S(2)}) async-start(bf16[8,256,1792]{2,1,0:T(8,128)(2,1)} %stack.8), calls=%async_computation | async-start | bytes 14680064 | tf_op jit(solution)/shard_map/all_to_all | solution.py:55
  48.7 254.2 %reduce-scatter.2.cloned.1.call-start = ((), (), s32[]{:S(2)}) async-start(), calls=%async_computation.3 | async-start | bytes 8257536 | tf_op jit(solution)/shard_map/reduce_scatter | solution.py:67
  56.5 4.3 %collective-permute-start.3 = (bf16[256,2048]{0,1:T(8,128)(2,1)}, bf16[256,2048]{0,1:T(8,128)(2,1)S(1)}, u32[]{:S(2)}, u32[]{:S(2)}) collective-permute-start(bf16[256,2048]{0,1:T(8,128)(2,1)} %bitcast.11), channel_id=1, source_target_pairs={{0,8},{8,0},{1,9},{9,1},{2,10},{10,2},{3,11},{11,3},{4,12},{12,4},... | collective-permute-start | bytes 3145736 | tf_op jit(solution)/shard_map/ppermute | solution.py:51
  56.5 4.3 %collective-permute-start.1 = (bf16[256,1792]{1,0:T(8,128)(2,1)}, bf16[256,1792]{1,0:T(8,128)(2,1)}, u32[]{:S(2)}, u32[]{:S(2)}) collective-permute-start(bf16[256,1792]{1,0:T(8,128)(2,1)} %param.5), channel_id=1, source_target_pairs={{0,8},{8,0},{1,9},{9,1},{2,10},{10,2},{3,11},{11,3},{4,12},{12,4},... | collective-permute-start | bytes 2752520 | tf_op jit(solution)/shard_map/ppermute | solution.py:52
  275.5 12.6 %collective-permute-start.2 = (bf16[256,2048]{0,1:T(8,128)(2,1)S(1)}, bf16[256,2048]{0,1:T(8,128)(2,1)S(1)}, u32[]{:S(2)}, u32[]{:S(2)}) collective-permute-start(bf16[256,2048]{0,1:T(8,128)(2,1)S(1)} %fusion.1), channel_id=1, source_target_pairs={{0,8},{8,0},{1,9},{9,1},{2,10},{10,2},{3,11},{11,3},{4,12},{12,4},... | collective-permute-start | bytes 3145736 | tf_op jit(solution)/shard_map/ppermute | solution.py:79
  282.4 25.5 %collective-permute-start.4 = (f32[256,1792]{1,0:T(8,128)}, f32[256,1792]{1,0:T(8,128)}, u32[]{:S(2)}, u32[]{:S(2)}) collective-permute-start(f32[256,1792]{1,0:T(8,128)} %fusion.10), channel_id=1, source_target_pairs={{0,8},{8,0},{1,9},{9,1},{2,10},{10,2},{3,11},{11,3},{4,12},{12,4},... | collective-permute-start | bytes 5505032 | tf_op jit(solution)/shard_map/ppermute | solution.py:92
  296.9 33.1 %all-to-all-start.1 = ((bf16[256,8,512]{2,0,1:T(8,128)(2,1)}), bf16[256,8,512]{2,0,1:T(8,128)(2,1)S(1)}, u32[]{:S(2)}, u32[]{:S(2)}) async-start(bf16[256,8,512]{2,0,1:T(8,128)(2,1)} %copy.25), calls=%async_computation.1 | async-start | bytes 4194304 | tf_op jit(solution)/shard_map/all_to_all | solution.py:88
  304.7 34.3 %collective-permute-start.5 = (bf16[128,1792]{1,0:T(8,128)(2,1)}, bf16[128,1792]{1,0:T(8,128)(2,1)}, u32[]{:S(2)}, u32[]{:S(2)}) collective-permute-start(bf16[128,1792]{1,0:T(8,128)(2,1)} %slice.19), channel_id=1, source_target_pairs={{0,16},{16,0},{1,17},{17,1},{2,18},{18,2},{3,19},{19,3},{4,20},{20... | collective-permute-start | bytes 1376264 | tf_op jit(solution)/shard_map/ppermute | solution.py:70
  314.5 24.5 %copy-start = (bf16[256,1792]{1,0:T(8,128)(2,1)S(1)}, bf16[256,1792]{1,0:T(8,128)(2,1)}, u32[]{:S(2)}) copy-start(bf16[256,1792]{1,0:T(8,128)(2,1)} %reduce-scatter.2.cloned.1.call-done) | copy-start | bytes 2752516
Sparse Core Ops, SparseCore 0:
  68.4 208.1 reduce-scatter.1
